TPU v7x, 32 devices: a whole 2x2x4 slice. The times are simulated.
32 devices in a mesh: groups: 2 (over x), tensor: 16 (over z, y, core).
Axes of the slice: x: 2, y: 2, z: 4, core: 2. Of those that a mesh axis runs over, the one named last changes fastest.
Arguments:
- tokens: bfloat16 [256, 8192], P(('groups', 'tensor')), parts along dimension 0, may hold values from -6 to 6
- gate_weight: bfloat16 [8192, 28672], P(None, 'tensor'), may hold values from -0.0625 to 0.0625
- up_weight: bfloat16 [8192, 28672], P(None, 'tensor'), may hold values from -0.0625 to 0.0625
- adapter_down_weight: bfloat16 [16, 8192, 64], P('tensor'), may hold values from -0.0625 to 0.0625
- adapter_up_weight: bfloat16 [16, 64, 28672], P(None, None, 'tensor'), may hold values from -0.75 to 0.75
- token_adapter_index: int32 [256, 1], P(('groups', 'tensor')), parts along dimension 0, may hold values from 0 to 15; in each aligned block of 128 rows (0 to 127, 128 to 255, ...) at most 16 rows name the same one
- adapter_slot_index: int32 [16], replicated, may hold values from 0 to 15, each once
Outputs:
- hidden: bfloat16 [256, 28672], P('groups', 'tensor'), parts along dimension 0
There are 2 independent parts, one for each index of `groups`. A program takes and returns all parts, laid end to end along the dimension named above; an argument that names none is the same for every part. Nothing has to cross between parts.
Inputs may be any that keep to these rules, and one draw needn't show every extreme that they name: `token_adapter_index`: in every draw at most 16 of all 128 tokens use one adapter, and some adapter is used by exactly 16 tokens; every adapter is used by some token. `adapter_slot_index`: A permutation; slot s is stored on the device of index s along tensor.
All inputs are finite; a program needn't handle non-finite values.
Results may differ from a plain program's by a relative error of at most 0.0039.
Values may be sent and summed in bfloat16 or wider, within the bound.
No kernel may reach another device: no remote copies, remote signals or barrier semaphores. Data moves between devices by JAX's collectives and lax.ppermute only.
A program may use at most 192 MiB of HBM per device.

v0:
```python
import jax
import jax.numpy as jnp
from jax import lax
from jax.sharding import PartitionSpec as P

CHUNKS = 2
LANES = 128


def body(
    tokens,
    gate_weight,
    up_weight,
    adapter_down_weight,
    adapter_up_weight,
    token_adapter_index,
    adapter_slot_index,
):
    me = lax.axis_index("tensor")
    rows, width = tokens.shape
    step = width // CHUNKS
    local_slot = jnp.take(adapter_slot_index, token_adapter_index[:, 0], axis=0)
    slot_cols = jnp.broadcast_to(local_slot.astype(jnp.bfloat16)[:, None], (rows, LANES))
    gate = up = low = None
    slots = None
    for c in range(CHUNKS):
        piece = tokens[:, c * step : (c + 1) * step]
        if c == CHUNKS - 1:
            piece = jnp.concatenate([piece, slot_cols], axis=1)
        gathered = lax.all_gather(piece, "tensor", axis=0, tiled=True)
        if c == CHUNKS - 1:
            slots = gathered[:, step].astype(jnp.int32)
            gathered = gathered[:, :step]
        g = jnp.dot(
            gathered, gate_weight[c * step : (c + 1) * step], preferred_element_type=jnp.float32
        )
        u = jnp.dot(
            gathered, up_weight[c * step : (c + 1) * step], preferred_element_type=jnp.float32
        )
        d = jnp.dot(
            gathered,
            adapter_down_weight[0, c * step : (c + 1) * step],
            preferred_element_type=jnp.float32,
        )
        gate = g if gate is None else gate + g
        up = u if up is None else up + u
        low = d if low is None else low + d
    mine = slots == me
    low = jnp.where(mine[:, None], low, 0.0).astype(jnp.bfloat16)
    spread = lax.all_gather(low, "tensor", axis=0, tiled=False)
    delta = jnp.einsum("str,srh->th", spread, adapter_up_weight, preferred_element_type=jnp.float32)
    return (jax.nn.silu(gate) * (up + delta)).astype(jnp.bfloat16)


def solution(mesh):
    in_specs = (
        P(("groups", "tensor"), None),
        P(None, "tensor"),
        P(None, "tensor"),
        P("tensor", None, None),
        P(None, None, "tensor"),
        P(("groups", "tensor"), None),
        P(),
    )
    out_specs = P("groups", "tensor")
    return jax.shard_map(body, mesh=mesh, in_specs=in_specs, out_specs=out_specs, check_vma=False)
```

profile of v0, /device:TPU:0, one launch (start us, length us, event | category | flops | bytes accessed | tf_op | source)
XLA Modules:
  0.0 148.9 jit_solution(2792847004383480132)
XLA Ops:
  6.5 0.0 copy-start
  6.5 0.0 all-gather.4.cloned.1.call-start
  6.5 1.5 %fusion.40 = (bf16[8,4096]{1,0:T(8,128)(2,1)}, bf16[8,4096]{1,0:T(8,128)(2,1)S(1)}) fusion(bf16[8,8192]{1,0:T(8,128)(2,1)} %param.7), kind=kLoop, calls=%fused_computation.36 | loop fusion | bytes 262144 | tf_op jit(solution)/shard_map/slice | solution.py:27
  8.0 0.0 all-gather.4.cloned.1.call-update
  8.1 0.0 all-gather.6.cloned.1.call-start
  8.1 0.7 fusion.39
  8.8 0.0 copy-done
  8.8 0.6 gather_fusion
  9.4 0.7 convert_bitcast_fusion
  10.1 0.1 broadcast_in_dim.26
  10.2 0.6 pad_maximum_fusion
  10.8 0.0 all-gather.6.cloned.1.call-update
  10.8 39.3 %all-gather.4.cloned.1.call-done = bf16[128,4096]{1,0:T(8,128)(2,1)} async-done(((bf16[8,4096]{1,0:T(8,128)(2,1)}), bf16[128,4096]{1,0:T(8,128)(2,1)}) %all-gather.4.cloned.1.call-update) | async-done | bytes 1048592 | tf_op jit(solution)/shard_map/all_gather | solution.py:30
  50.2 1.8 %fusion.34 = f32[128,64]{0,1:T(8,128)S(1)} fusion(bf16[128,4096]{1,0:T(8,128)(2,1)} %all-gather.4.cloned.1.call-done, bf16[1,8192,64]{1,2,0:T(8,128)(2,1)} %param.10), kind=kOutput, calls=%fused_computation.24 | convolution fusion | flops 67108864 | bytes 1605632 | tf_op jit(solution)/shard_map/dot_general | solution.py:40
  52.0 37.4 %all-gather.6.cloned.1.call-done = bf16[128,4224]{1,0:T(8,128)(2,1)} async-done(((bf16[8,4224]{1,0:T(8,128)(2,1)}), bf16[128,4224]{1,0:T(8,128)(2,1)}) %all-gather.6.cloned.1.call-update) | async-done | bytes 1081360 | tf_op jit(solution)/shard_map/all_gather | solution.py:30
  89.4 0.0 copy-start.3
  89.4 1.0 fusion.38
  90.4 1.8 %fusion.29 = bf16[128,64]{0,1:T(8,128)(2,1)S(1)} fusion(f32[128,64]{0,1:T(8,128)S(1)} %fusion.34, bf16[128,4224]{1,0:T(8,128)(2,1)} %all-gather.6.cloned.1.call-done, bf16[1,8192,64]{1,2,0:T(8,128)(2,1)} %param.10, pred[128]{0:T(512)(128)(4,1)S(1)} %fusion.38), kind=kOutput, calls=%fused_computation.19 | convolution fusion | flops 67133440 | bytes 1622144 | tf_op jit(solution)/shard_map/dot_general | solution.py:40
  92.2 20.1 %all-gather = bf16[2048,64]{0,1:T(8,128)(2,1)S(1)} all-gather(bf16[128,64]{0,1:T(8,128)(2,1)S(1)} %fusion.29), channel_id=2, replica_groups=mesh['groups'=2,'tensor'=16] {'tensor'}, dimensions={0}, use_global_device_ids=true | all-gather | bytes 278528 | tf_op jit(solution)/shard_map/all_gather | solution.py:50
  112.4 6.8 %fusion = f32[128,1792]{1,0:T(8,128)S(1)} fusion(bf16[8192,1792]{1,0:T(8,128)(2,1)} %param.9, bf16[128,4224]{1,0:T(8,128)(2,1)} %all-gather.6.cloned.1.call-done), kind=kOutput, calls=%fused_computation.1 | convolution fusion | flops 1879048192 | bytes 16646144 | tf_op jit(solution)/shard_map/dot_general | solution.py:37
  119.2 0.0 copy-done.3
  119.2 0.0 copy-start.2
  119.2 6.5 %fusion.4 = f32[128,1792]{1,0:T(8,128)S(1)} fusion(bf16[8192,1792]{1,0:T(8,128)(2,1)} %param.8, bf16[128,4224]{1,0:T(8,128)(2,1)S(1)} %copy-done.3), kind=kOutput, calls=%fused_computation.5 | convolution fusion | flops 1879048192 | bytes 16646144 | tf_op jit(solution)/shard_map/dot_general | solution.py:34
  125.7 0.0 copy-done.2
  125.7 6.5 %fusion.13 = f32[128,1792]{1,0:T(8,128)S(1)} fusion(f32[128,1792]{1,0:T(8,128)S(1)} %fusion.4, bf16[128,4096]{1,0:T(8,128)(2,1)S(1)} %copy-done.2, bf16[8192,1792]{1,0:T(8,128)(2,1)} %param.8), kind=kOutput, calls=%fused_computation.12 | convolution fusion | flops 1879277568 | bytes 17563648 | tf_op jit(solution)/shard_map/dot_general | solution.py:34
  132.2 0.0 copy-start.4
  132.2 0.0 copy-start.1
  132.2 6.6 %fusion.16 = f32[128,1792]{1,0:T(8,128)S(1)} fusion(f32[128,1792]{1,0:T(8,128)S(1)} %fusion, bf16[128,4096]{1,0:T(8,128)(2,1)S(1)} %copy-done.2, bf16[8192,1792]{1,0:T(8,128)(2,1)} %param.9), kind=kOutput, calls=%fused_computation.13 | convolution fusion | flops 1879277568 | bytes 17563648 | tf_op jit(solution)/shard_map/dot_general | solution.py:37
  138.9 0.0 copy-done.4
  138.9 3.2 %fusion.25 = bf16[128,1792]{1,0:T(8,128)(2,1)} fusion(f32[128,1792]{1,0:T(8,128)S(1)} %fusion.16, bf16[16,128,64]{1,0,2:T(8,128)(2,1)S(1)} %bitcast.31, bf16[16,64,1792]{2,1,0:T(8,128)(2,1)S(1)} %copy-done.4, f32[128,1792]{1,0:T(8,128)S(1)} %fusion.13), kind=kOutput, calls=%fused_computation.16 | convolution fusion | flops 471367680 | bytes 6225920 | tf_op jit(solution)/shard_map/str,srh->th/dot_general | solution.py:51
  142.1 0.0 copy-done.1
  (2 shorter events, 0.0 us)
Async XLA Ops:
  6.5 2.3 %copy-start = (s32[16]{0:T(128)S(1)}, s32[16]{0:T(128)}, u32[]{:S(2)}) copy-start(s32[16]{0:T(128)} %param.13) | copy-start | bytes 196
  6.5 43.7 %all-gather.4.cloned.1.call-start = ((), (), s32[]{:S(2)}) async-start(), calls=%async_computation | async-start | bytes 1114112 | tf_op jit(solution)/shard_map/all_gather | solution.py:30
  8.1 81.3 %all-gather.6.cloned.1.call-start = ((), (), s32[]{:S(2)}) async-start(), calls=%async_computation.1 | async-start | bytes 1148928 | tf_op jit(solution)/shard_map/all_gather | solution.py:30
  89.4 29.8 %copy-start.3 = (bf16[128,4224]{1,0:T(8,128)(2,1)S(1)}, bf16[128,4224]{1,0:T(8,128)(2,1)}, u32[]{:S(2)}) copy-start(bf16[128,4224]{1,0:T(8,128)(2,1)} %all-gather.6.cloned.1.call-done) | copy-start | bytes 3244036
  119.2 6.6 %copy-start.2 = (bf16[128,4096]{1,0:T(8,128)(2,1)S(1)}, bf16[128,4096]{1,0:T(8,128)(2,1)}, u32[]{:S(2)}) copy-start(bf16[128,4096]{1,0:T(8,128)(2,1)} %all-gather.4.cloned.1.call-done) | copy-start | bytes 3145732
  132.2 6.7 %copy-start.4 = (bf16[16,64,1792]{2,1,0:T(8,128)(2,1)S(1)}, bf16[16,64,1792]{2,1,0:T(8,128)(2,1)}, u32[]{:S(2)}) copy-start(bf16[16,64,1792]{2,1,0:T(8,128)(2,1)} %param.11) | copy-start | bytes 11010052
  132.2 9.8 %copy-start.1 = (s32[16]{0:T(128)S(1)}, s32[16]{0:T(128)}, u32[]{:S(2)}) copy-start(s32[16]{0:T(128)} %param.13) | copy-start | bytes 196
Sparse Core Ops, SparseCore 0:
  9.5 40.6 all-gather.3
  52.4 36.9 all-gather.5
where the time goes:
time: 149 us
  waiting for transfers between devices  76.7 us (51%)
  matrix products  33.3 us (22%)
  blocking collectives  20.1 us (13%)
  between operations  13.5 us (9%)
  other arithmetic  2.93 us (2%)
  local copies, waits for them, and re-layouts  2.29 us (2%)
    all_gather x2, waiting for transfers between devices, body(): gathered = lax.all_gather(piece, 'tensor', axis=0, tiled=True)  76.7 us
    all_gather x1, blocking collectives, body(): spread = lax.all_gather(low, 'tensor', axis=0, tiled=False)  20.1 us
    dot_general x2, matrix products, body(): jnp.dot(gathered, up_weight[c * step:(c + 1) * step], preferred_element_t...  13.4 us
    dot_general x2, matrix products, body(): jnp.dot(gathered, gate_weight[c * step:(c + 1) * step], preferred_element...  13 us
    dot_general x2, matrix products, body(): jnp.dot(gathered, adapter_down_weight[0, c * step:(c + 1) * step], prefer...  3.68 us
    dot_general x1, matrix products, body(): jnp.einsum('str,srh->th', spread, adapter_up_weight, preferred_element_ty...  3.19 us
  transfers between devices with their start and end apart: 2, of which 2 were waited for; matrix products, arithmetic and copies ran while one was open for 3% of the time, Pallas kernels for 0%

commit v1 on v0

--- a/solution.py
+++ b/solution.py
@@ -27,7 +27,22 @@
         piece = tokens[:, c * step : (c + 1) * step]
         if c == CHUNKS - 1:
             piece = jnp.concatenate([piece, slot_cols], axis=1)
-        gathered = lax.all_gather(piece, "tensor", axis=0, tiled=True)
+
+        def deliver_state(array_in):
+            z2 = lax.axis_index("tensor")
+            s_next = lax.axis_size("tensor")
+            a_next, answer = (s_next, z2)
+            plain, formed = (array_in, 1)
+            while formed < a_next:
+                everything = tuple(((pp, pp ^ formed) for pp in range(a_next)))
+                y = lax.ppermute(plain, "tensor", everything)
+                seen_now = jnp.concatenate([plain, y], axis=0)
+                piece_next = jnp.concatenate([y, plain], axis=0)
+                plain = jnp.where(answer & formed == 0, seen_now, piece_next)
+                formed = 2 * formed
+            return plain
+
+        gathered = deliver_state(piece)
         if c == CHUNKS - 1:
             slots = gathered[:, step].astype(jnp.int32)
             gathered = gathered[:, :step]

time: 149 us -> 119 us (0.80)
  waiting for transfers between devices: 76.7 us -> 53.9 us
  between operations: 13.5 us -> 0.15 us
  starting transfers between devices: 0.04 us -> 8.87 us
  matrix products: 33.3 us -> 30.3 us
  blocking collectives: 20.1 us -> 21.7 us
    all_gather x2 -> x0, waiting for transfers between devices: 76.7 us -> none  [body(): gathered = lax.all_gather(piece, 'tensor', axis=0, tiled=True)]
    ppermute x0 -> x8, waiting for transfers between devices: none -> 53.9 us  [deliver_state(): y = lax.ppermute(plain, 'tensor', everything)]
    ppermute x0 -> x8, starting transfers between devices: none -> 8.87 us  [deliver_state(): y = lax.ppermute(plain, 'tensor', everything)]
    dot_general x2, matrix products: 3.68 us -> 0.99 us  [body(): jnp.dot(gathered, adapter_down_weight[0, c * step:(c + 1) * step], prefer...]
    all_gather x1, blocking collectives: 20.1 us -> 21.7 us  [body(): spread = lax.all_gather(low, 'tensor', axis=0, tiled=False)]
  transfers between devices with their start and end apart: 2 -> 8, of which waited for: 2 -> 7; matrix products, arithmetic and copies ran while one was open for 3% -> 1% of each run, Pallas kernels for 0% -> 0%
where the time goes in v1:
time: 119 us
  waiting for transfers between devices  53.9 us (45%)
  matrix products  30.3 us (25%)
  blocking collectives  21.7 us (18%)
  starting transfers between devices  8.87 us (7%)
  other arithmetic  1.97 us (2%)
  local copies, waits for them, and re-layouts  1.66 us (1%)
    ppermute x8, waiting for transfers between devices, deliver_state(): y = lax.ppermute(plain, 'tensor', everything)  53.9 us
    all_gather x1, blocking collectives, body(): spread = lax.all_gather(low, 'tensor', axis=0, tiled=False)  21.7 us
    dot_general x2, matrix products, body(): jnp.dot(gathered, up_weight[c * step:(c + 1) * step], preferred_element_t...  13.9 us
    dot_general x2, matrix products, body(): jnp.dot(gathered, gate_weight[c * step:(c + 1) * step], preferred_element...  13.1 us
    ppermute x8, starting transfers between devices, deliver_state(): y = lax.ppermute(plain, 'tensor', everything)  8.87 us
  transfers between devices with their start and end apart: 8, of which 7 were waited for; matrix products, arithmetic and copies ran while one was open for 1% of the time, Pallas kernels for 0%

profile of v1, /device:TPU:0, one launch (start us, length us, event | category | flops | bytes accessed | tf_op | source)
XLA Modules:
  0.0 118.5 jit_solution(3599388652628064634)
XLA Ops:
  0.0 0.0 copy-start
  0.0 0.7 fusion.33
  0.7 0.0 copy-done
  0.7 0.6 gather_fusion
  1.3 0.7 convert_bitcast_fusion
  2.0 0.9 fusion.36
  2.9 0.1 broadcast_in_dim.26
  3.0 0.5 collective-permute-start.4
  3.4 0.1 collective-permute-start
  3.5 0.8 collective-permute-done.4
  4.4 2.9 %collective-permute-start.5 = (bf16[16,4224]{1,0:T(8,128)(2,1)S(1)}, bf16[16,4224]{1,0:T(8,128)(2,1)S(1)}, u32[]{:S(2)}, u32[]{:S(2)}) collective-permute-start(bf16[16,4224]{1,0:T(8,128)(2,1)S(1)} %maximum_select_fusion.6), channel_id=1, source_target_pairs={{0,2},{1,3},{2,0},{3,1},{4,6},{5,7},{6,4},{7,5},{8,10},{9,11},{10,... | collective-permute-start | bytes 405512 | tf_op jit(solution)/shard_map/ppermute | solution.py:38
  7.3 0.0 collective-permute-done
  7.3 0.1 collective-permute-start.1
  7.5 4.2 %collective-permute-done.5 = bf16[16,4224]{1,0:T(8,128)(2,1)S(1)} collective-permute-done((bf16[16,4224]{1,0:T(8,128)(2,1)S(1)}, bf16[16,4224]{1,0:T(8,128)(2,1)S(1)}, u32[]{:S(2)}, u32[]{:S(2)}) %collective-permute-start.5) | collective-permute-done | bytes 135200 | tf_op jit(solution)/shard_map/ppermute | solution.py:38
  11.7 2.2 %collective-permute-start.6 = (bf16[32,4224]{1,0:T(8,128)(2,1)S(1)}, bf16[32,4224]{1,0:T(8,128)(2,1)S(1)}, u32[]{:S(2)}, u32[]{:S(2)}) collective-permute-start(bf16[32,4224]{1,0:T(8,128)(2,1)S(1)} %maximum_select_fusion.4), channel_id=1, source_target_pairs={{0,4},{1,5},{2,6},{3,7},{4,0},{5,1},{6,2},{7,3},{8,12},{9,13},{10,... | collective-permute-start | bytes 811016 | tf_op jit(solution)/shard_map/ppermute | solution.py:38
  13.9 0.1 collective-permute-done.1
  14.1 0.0 copy-start.3
  14.1 1.9 %collective-permute-start.2 = (bf16[32,4096]{1,0:T(8,128)(2,1)S(1)}, bf16[32,4096]{1,0:T(8,128)(2,1)S(1)}, u32[]{:S(2)}, u32[]{:S(2)}) collective-permute-start(bf16[32,4096]{1,0:T(8,128)(2,1)S(1)} %maximum_select_fusion.5), channel_id=1, source_target_pairs={{0,4},{1,5},{2,6},{3,7},{4,0},{5,1},{6,2},{7,3},{8,12},{9,13},{10,... | collective-permute-start | bytes 786440 | tf_op jit(solution)/shard_map/ppermute | solution.py:38
  15.9 8.7 %collective-permute-done.6 = bf16[32,4224]{1,0:T(8,128)(2,1)S(1)} collective-permute-done((bf16[32,4224]{1,0:T(8,128)(2,1)S(1)}, bf16[32,4224]{1,0:T(8,128)(2,1)S(1)}, u32[]{:S(2)}, u32[]{:S(2)}) %collective-permute-start.6) | collective-permute-done | bytes 270368 | tf_op jit(solution)/shard_map/ppermute | solution.py:38
  24.6 0.1 maximum_select_fusion.2
  24.7 1.2 collective-permute-start.7
  25.9 4.9 %collective-permute-done.2 = bf16[32,4096]{1,0:T(8,128)(2,1)S(1)} collective-permute-done((bf16[32,4096]{1,0:T(8,128)(2,1)S(1)}, bf16[32,4096]{1,0:T(8,128)(2,1)S(1)}, u32[]{:S(2)}, u32[]{:S(2)}) %collective-permute-start.2) | collective-permute-done | bytes 262176 | tf_op jit(solution)/shard_map/ppermute | solution.py:38
  30.8 0.1 maximum_select_fusion.3
  30.9 0.1 collective-permute-start.3
  30.9 30.3 %collective-permute-done.7 = bf16[64,4224]{1,0:T(8,128)(2,1)S(1)} collective-permute-done((bf16[64,4224]{1,0:T(8,128)(2,1)S(1)}, bf16[64,4224]{1,0:T(8,128)(2,1)S(1)}, u32[]{:S(2)}, u32[]{:S(2)}) %collective-permute-start.7) | collective-permute-done | bytes 540704 | tf_op jit(solution)/shard_map/ppermute | solution.py:38
  61.2 0.2 maximum_select_fusion
  61.4 0.1 fusion.32
  61.5 0.0 copy-done.3
  61.5 0.5 fusion.24
  62.0 4.8 %collective-permute-done.3 = bf16[64,4096]{1,0:T(8,128)(2,1)S(1)} collective-permute-done((bf16[64,4096]{1,0:T(8,128)(2,1)S(1)}, bf16[64,4096]{1,0:T(8,128)(2,1)S(1)}, u32[]{:S(2)}, u32[]{:S(2)}) %collective-permute-start.3) | collective-permute-done | bytes 524320 | tf_op jit(solution)/shard_map/ppermute | solution.py:38
  66.9 0.5 fusion.23
  67.4 21.7 %all-gather = bf16[2048,64]{0,1:T(8,128)(2,1)S(1)} all-gather(bf16[128,64]{0,1:T(8,128)(2,1)S(1)} %fusion.23), channel_id=2, replica_groups=mesh['groups'=2,'tensor'=16] {'tensor'}, dimensions={0}, use_global_device_ids=true | all-gather | bytes 278528 | tf_op jit(solution)/shard_map/all_gather | solution.py:65
  89.1 6.5 %fusion = f32[128,1792]{1,0:T(8,128)S(1)} fusion(bf16[8192,1792]{1,0:T(8,128)(2,1)} %param.9, bf16[128,4224]{1,0:T(8,128)(2,1)S(1)} %maximum_select_fusion), kind=kOutput, calls=%fused_computation.1 | convolution fusion | flops 1879048192 | bytes 16646144 | tf_op jit(solution)/shard_map/dot_general | solution.py:52
  95.6 0.0 copy-start.2
  95.6 6.6 %fusion.4 = f32[128,1792]{1,0:T(8,128)S(1)} fusion(bf16[8192,1792]{1,0:T(8,128)(2,1)} %param.8, bf16[128,4224]{1,0:T(8,128)(2,1)S(1)} %maximum_select_fusion), kind=kOutput, calls=%fused_computation.5 | convolution fusion | flops 1879048192 | bytes 16646144 | tf_op jit(solution)/shard_map/dot_general | solution.py:49
  102.2 0.0 copy-done.2
  102.2 2.3 %fusion.10 = f32[128,1792]{1,0:T(8,128)S(1)} fusion(bf16[16,128,64]{1,0,2:T(8,128)(2,1)S(1)} %bitcast.21, bf16[16,64,1792]{2,1,0:T(8,128)(2,1)S(1)} %copy-done.2), kind=kOutput, calls=%fused_computation.11 | convolution fusion | flops 469762048 | bytes 4849664 | tf_op jit(solution)/shard_map/str,srh->th/dot_general | solution.py:66
  104.6 6.5 %fusion.13 = f32[128,1792]{1,0:T(8,128)S(1)} fusion(f32[128,1792]{1,0:T(8,128)S(1)} %fusion.4, bf16[8192,1792]{1,0:T(8,128)(2,1)} %param.8, bf16[64,4096]{1,0:T(8,128)(2,1)S(1)} %collective-permute-done.3, bf16[64,4096]{1,0:T(8,128)(2,1)S(1)} %maximum_select_fusion.3, pred[]{:T(512)S(6)} %eq.23), kind=kOutput, calls=%fused_computation.12 | convolution fusion | flops 1883996160 | bytes 17563648 | tf_op jit(solution)/shard_map/dot_general | solution.py:49
  111.1 0.0 copy-start.1
  111.1 7.4 %multiply_convert_fusion = bf16[128,1792]{1,0:T(8,128)(2,1)} fusion(f32[128,1792]{1,0:T(8,128)S(1)} %fusion.13, f32[128,1792]{1,0:T(8,128)S(1)} %fusion.10, f32[128,1792]{1,0:T(8,128)S(1)} %fusion, bf16[8192,1792]{1,0:T(8,128)(2,1)} %param.9, bf16[64,4096]{1,0:T(8,128)(2,1)S(1)} %collective-permute-done.3, bf16[64,4096]{1,0:T(8,128)(2,1)S(1)} %maximum_select_fusion.3, ...), kind=kOutput, calls=%fused_computation.20 | convolution fusion | flops 1885601792 | bytes 18939904 | tf_op jit(solution)/shard_map/dot_general | solution.py:52
  118.5 0.0 copy-done.1
  (7 shorter events, 0.2 us)
Async XLA Ops:
  0.0 0.7 copy-start
  3.0 1.4 %collective-permute-start.4 = (bf16[8,4224]{1,0:T(8,128)(2,1)S(1)}, bf16[8,4224]{1,0:T(8,128)(2,1)S(1)}, u32[]{:S(2)}, u32[]{:S(2)}) collective-permute-start(bf16[8,4224]{1,0:T(8,128)(2,1)S(1)} %pad_maximum_fusion), channel_id=1, source_target_pairs={{0,1},{1,0},{2,3},{3,2},{4,5},{5,4},{6,7},{7,6},{8,9},{9,8},{10,11... | collective-permute-start | bytes 202760 | tf_op jit(solution)/shard_map/ppermute | solution.py:38
  3.4 3.9 %collective-permute-start = (bf16[8,4096]{1,0:T(8,128)(2,1)S(1)}, bf16[8,4096]{1,0:T(8,128)(2,1)S(1)}, u32[]{:S(2)}, u32[]{:S(2)}) collective-permute-start(bf16[8,4096]{1,0:T(8,128)(2,1)S(1)} %get-tuple-element.5), channel_id=1, source_target_pairs={{0,1},{1,0},{2,3},{3,2},{4,5},{5,4},{6,7},{7,6},{8,9},{9,8},{10,11... | collective-permute-start | bytes 196616 | tf_op jit(solution)/shard_map/ppermute | solution.py:38
  4.4 7.3 %collective-permute-start.5 = (bf16[16,4224]{1,0:T(8,128)(2,1)S(1)}, bf16[16,4224]{1,0:T(8,128)(2,1)S(1)}, u32[]{:S(2)}, u32[]{:S(2)}) collective-permute-start(bf16[16,4224]{1,0:T(8,128)(2,1)S(1)} %maximum_select_fusion.6), channel_id=1, source_target_pairs={{0,2},{1,3},{2,0},{3,1},{4,6},{5,7},{6,4},{7,5},{8,10},{9,11},{10,... | collective-permute-start | bytes 405512 | tf_op jit(solution)/shard_map/ppermute | solution.py:38
  7.3 6.7 %collective-permute-start.1 = (bf16[16,4096]{1,0:T(8,128)(2,1)S(1)}, bf16[16,4096]{1,0:T(8,128)(2,1)S(1)}, u32[]{:S(2)}, u32[]{:S(2)}) collective-permute-start(bf16[16,4096]{1,0:T(8,128)(2,1)S(1)} %maximum_select_fusion.7), channel_id=1, source_target_pairs={{0,2},{1,3},{2,0},{3,1},{4,6},{5,7},{6,4},{7,5},{8,10},{9,11},{10,... | collective-permute-start | bytes 393224 | tf_op jit(solution)/shard_map/ppermute | solution.py:38
  11.7 12.9 %collective-permute-start.6 = (bf16[32,4224]{1,0:T(8,128)(2,1)S(1)}, bf16[32,4224]{1,0:T(8,128)(2,1)S(1)}, u32[]{:S(2)}, u32[]{:S(2)}) collective-permute-start(bf16[32,4224]{1,0:T(8,128)(2,1)S(1)} %maximum_select_fusion.4), channel_id=1, source_target_pairs={{0,4},{1,5},{2,6},{3,7},{4,0},{5,1},{6,2},{7,3},{8,12},{9,13},{10,... | collective-permute-start | bytes 811016 | tf_op jit(solution)/shard_map/ppermute | solution.py:38
  14.1 47.5 %copy-start.3 = (bf16[1,8192,64]{1,2,0:T(8,128)(2,1)S(1)}, bf16[1,8192,64]{1,2,0:T(8,128)(2,1)}, u32[]{:S(2)}) copy-start(bf16[1,8192,64]{1,2,0:T(8,128)(2,1)} %param.10) | copy-start | bytes 3145732
  14.1 16.7 %collective-permute-start.2 = (bf16[32,4096]{1,0:T(8,128)(2,1)S(1)}, bf16[32,4096]{1,0:T(8,128)(2,1)S(1)}, u32[]{:S(2)}, u32[]{:S(2)}) collective-permute-start(bf16[32,4096]{1,0:T(8,128)(2,1)S(1)} %maximum_select_fusion.5), channel_id=1, source_target_pairs={{0,4},{1,5},{2,6},{3,7},{4,0},{5,1},{6,2},{7,3},{8,12},{9,13},{10,... | collective-permute-start | bytes 786440 | tf_op jit(solution)/shard_map/ppermute | solution.py:38
  24.7 36.5 %collective-permute-start.7 = (bf16[64,4224]{1,0:T(8,128)(2,1)S(1)}, bf16[64,4224]{1,0:T(8,128)(2,1)S(1)}, u32[]{:S(2)}, u32[]{:S(2)}) collective-permute-start(bf16[64,4224]{1,0:T(8,128)(2,1)S(1)} %maximum_select_fusion.2), channel_id=1, source_target_pairs={{0,8},{1,9},{2,10},{3,11},{4,12},{5,13},{6,14},{7,15},{8,0},{9,1},... | collective-permute-start | bytes 1622024 | tf_op jit(solution)/shard_map/ppermute | solution.py:38
  30.9 36.0 %collective-permute-start.3 = (bf16[64,4096]{1,0:T(8,128)(2,1)S(1)}, bf16[64,4096]{1,0:T(8,128)(2,1)S(1)}, u32[]{:S(2)}, u32[]{:S(2)}) collective-permute-start(bf16[64,4096]{1,0:T(8,128)(2,1)S(1)} %maximum_select_fusion.3), channel_id=1, source_target_pairs={{0,8},{1,9},{2,10},{3,11},{4,12},{5,13},{6,14},{7,15},{8,0},{9,1},... | collective-permute-start | bytes 1572872 | tf_op jit(solution)/shard_map/ppermute | solution.py:38
  95.6 6.6 %copy-start.2 = (bf16[16,64,1792]{2,1,0:T(8,128)(2,1)S(1)}, bf16[16,64,1792]{2,1,0:T(8,128)(2,1)}, u32[]{:S(2)}) copy-start(bf16[16,64,1792]{2,1,0:T(8,128)(2,1)} %param.11) | copy-start | bytes 11010052
  111.1 7.4 %copy-start.1 = (s32[16]{0:T(128)S(1)}, s32[16]{0:T(128)}, u32[]{:S(2)}) copy-start(s32[16]{0:T(128)} %param.13) | copy-start | bytes 196
